TPU v7x, 256 devices: a whole 4x4x8 slice. The times are simulated.
256 devices in a mesh: ctx: 32 (over x, z), tp: 8 (over y, core).
Axes of the slice: x: 4, y: 4, z: 8, core: 2. Of those that a mesh axis runs over, the one named last changes fastest.
Arguments:
- query_in: bfloat16 [16384, 4096], P('ctx', 'tp'), may hold values from -6 to 6
- key_in: bfloat16 [16384, 4096], P('ctx', 'tp'), may hold values from -6 to 6
- value_in: bfloat16 [16384, 4096], P('ctx', 'tp'), may hold values from -6 to 6
- out_grad: bfloat16 [16384, 4096], P('ctx', 'tp'), may hold values from -6 to 6
- doc_ids: int32 [16384], replicated, may hold values from 0 to 15, never falling along the last dimension, each value on 1 to 2048 neighbouring positions
- skip_gain: float32 [4096], P('tp'), may hold values from -4 to 4
- filter_taps: bfloat16 [2048, 8], P(('ctx', 'tp')), may hold values from -0.125 to 0.125
Outputs:
- mixed_out: bfloat16 [16384, 4096], P('ctx', 'tp')
- query_grad: bfloat16 [16384, 4096], P('ctx', 'tp')
- key_grad: bfloat16 [16384, 4096], P('ctx', 'tp')
- value_grad: bfloat16 [16384, 4096], P('ctx', 'tp')
- filter_grad: float32 [2048, 8], P(('ctx', 'tp'))
Inputs may be any that keep to these rules, and one draw needn't show every extreme that they name: `doc_ids`: ids never fall along the tokens; each document is 1 to 2048 tokens long and one is exactly 2048 long.
All inputs are finite; a program needn't handle non-finite values.
Results may differ from a plain program's by a relative error of at most 0.0049.
Values may be sent and summed in bfloat16 or wider, within the bound.
No kernel may reach another device: no remote copies, remote signals or barrier semaphores. Data moves between devices by JAX's collectives and lax.ppermute only.
A program may use at most 128 MiB of HBM per device.

v0:
```python
import math
import jax
import jax.numpy as jnp
from jax import lax
from jax.sharding import PartitionSpec as P

MAXCH = 8
FGROUP = 512
FLEN = 2048


def shifted(value, axis, steps):
    count = lax.axis_size(axis)
    leading, last = (max(0, -steps), min(count, count - steps))
    return lax.ppermute(value, axis, [(source, source + steps) for source in range(leading, last)])


def band(window, rows, cols):
    groups_n = window.shape[0]
    flat = jnp.tile(window, (1, rows))[:, : rows * cols]
    return flat.reshape(groups_n, rows, cols)


def shards(query_in, key_in, value_in, out_grad, doc_ids, skip_gain, filter_taps):
    rows, width = query_in.shape
    groups_here = width // FGROUP
    here = lax.axis_index("ctx")
    span = -(-FLEN // rows)
    hist = span * rows
    wide = hist + rows
    assert hist == FLEN
    full_taps = lax.all_gather(filter_taps, ("ctx", "tp"), axis=0, tiled=True)
    first_group = lax.axis_index("tp") * groups_here
    taps = lax.dynamic_slice_in_dim(full_taps, first_group, groups_here, axis=1).T
    mixed_in = (key_in.astype(jnp.float32) * value_in.astype(jnp.float32)).astype(jnp.bfloat16)
    conv_grad = (out_grad.astype(jnp.float32) * query_in.astype(jnp.float32)).astype(jnp.bfloat16)
    ahead = [mixed_in]
    behind = [conv_grad]
    for _ in range(span):
        ahead.append(shifted(ahead[-1], "ctx", 1))
        behind.append(shifted(behind[-1], "ctx", -1))
    sources = jnp.concatenate(ahead[::-1], axis=0).reshape(wide, groups_here, FGROUP)
    readers = jnp.concatenate(behind, axis=0).reshape(wide, groups_here, FGROUP)
    ids_pad = jnp.concatenate(
        [jnp.full((hist,), -1, jnp.int32), doc_ids, jnp.full((hist,), -2, jnp.int32)]
    )
    ids_own = lax.dynamic_slice_in_dim(doc_ids, here * rows, rows)
    ids_src = lax.dynamic_slice_in_dim(ids_pad, here * rows, wide)
    ids_rdr = lax.dynamic_slice_in_dim(ids_pad, here * rows + hist, wide)
    same_src = ids_own[:, None] == ids_src[None, :]
    same_rdr = ids_own[:, None] == ids_rdr[None, :]
    zero_taps = jnp.zeros((groups_here, wide + 1 - FLEN), taps.dtype)
    fwd_window = jnp.concatenate([zero_taps[:, :1], taps[:, ::-1], zero_taps[:, 1:]], axis=1)
    bwd_window = jnp.concatenate([taps, zero_taps], axis=1)
    fwd_tile = jnp.where(same_src[None], band(fwd_window, rows, wide), 0)
    bwd_tile = jnp.where(same_rdr[None], band(bwd_window, rows, wide), 0)
    skip = skip_gain.reshape(groups_here, FGROUP)
    own_src = mixed_in.reshape(rows, groups_here, FGROUP)
    own_grad = conv_grad.reshape(rows, groups_here, FGROUP)
    conv = skip * own_src.astype(jnp.float32) + jnp.einsum(
        "gab,bgc->agc", fwd_tile, sources, preferred_element_type=jnp.float32
    )
    mixed_grad = skip * own_grad.astype(jnp.float32) + jnp.einsum(
        "gab,bgc->agc", bwd_tile, readers, preferred_element_type=jnp.float32
    )
    product = jnp.einsum("agc,bgc->gab", own_grad, sources, preferred_element_type=jnp.float32)
    product = jnp.where(same_src[None], product, 0.0)
    skewed = jnp.pad(product.reshape(groups_here, rows * wide), ((0, 0), (0, rows)))
    diag = jnp.sum(skewed.reshape(groups_here, rows, wide + 1), axis=1)
    filter_part = diag[:, 1 : hist + 1][:, ::-1]
    conv = conv.reshape(rows, width)
    mixed_grad = mixed_grad.reshape(rows, width)
    mixed_out = (query_in.astype(jnp.float32) * conv).astype(jnp.bfloat16)
    query_grad = (out_grad.astype(jnp.float32) * conv).astype(jnp.bfloat16)
    key_grad = (mixed_grad * value_in.astype(jnp.float32)).astype(jnp.bfloat16)
    value_grad = (mixed_grad * key_in.astype(jnp.float32)).astype(jnp.bfloat16)
    placed = jnp.zeros((FLEN, full_taps.shape[1]), jnp.float32)
    placed = lax.dynamic_update_slice_in_dim(placed, filter_part.T, first_group, axis=1)
    summed = lax.psum_scatter(placed, ("ctx", "tp"), scatter_dimension=0, tiled=True)
    tokens = lax.axis_size("ctx") * rows
    filter_grad = summed * (1.0 / math.sqrt(FGROUP * tokens))
    return (mixed_out, query_grad, key_grad, value_grad, filter_grad)


def solution(mesh):
    in_specs = (
        P("ctx", "tp"),
        P("ctx", "tp"),
        P("ctx", "tp"),
        P("ctx", "tp"),
        P(),
        P("tp"),
        P(("ctx", "tp"), None),
    )
    out_specs = (
        P("ctx", "tp"),
        P("ctx", "tp"),
        P("ctx", "tp"),
        P("ctx", "tp"),
        P(("ctx", "tp"), None),
    )
    return jax.shard_map(shards, mesh=mesh, in_specs=in_specs, out_specs=out_specs, check_vma=False)
```

profile of v0, /device:TPU:2, one launch (start us, length us, event | category | flops | bytes accessed | tf_op | source)
XLA Modules:
  0.0 723.5 jit_solution(13073037169013701247)
XLA Ops:
  7.2 1.3 copy.29
  8.5 1.4 copy.32
  9.9 1.0 constant_dynamic-update-slice_fusion.9
  10.9 7.7 %collective-permute-start.4 = (bf16[512,512]{0,1:T(8,128)(2,1)S(1)}, bf16[512,512]{0,1:T(8,128)(2,1)S(1)}, u32[]{:S(2)}, u32[]{:S(2)}) collective-permute-start(bf16[512,512]{0,1:T(8,128)(2,1)S(1)} %get-tuple-element.23), channel_id=1, source_target_pairs={{8,0},{16,8},{24,16},{32,24},{40,32},{48,40},{56,48},{64,56},{72,6... | collective-permute-start | bytes 1572872 | tf_op jit(solution)/shard_map/ppermute | solution.py:15
  18.7 0.1 fusion.13
  18.8 11.0 %collective-permute-done.4 = bf16[512,512]{0,1:T(8,128)(2,1)S(1)} collective-permute-done((bf16[512,512]{0,1:T(8,128)(2,1)S(1)}, bf16[512,512]{0,1:T(8,128)(2,1)S(1)}, u32[]{:S(2)}, u32[]{:S(2)}) %collective-permute-start.4) | collective-permute-done | bytes 524320 | tf_op jit(solution)/shard_map/ppermute | solution.py:15
  29.8 6.5 collective-permute-start.5
  36.3 5.3 broadcast_bitcast_fusion
  41.6 10.2 %copy.39 = s32[1,1,512,2560]{3,1,2,0:T(1,128)} copy(s32[1,1,512,2560]{3,2,1,0:T(8,128)} %get-tuple-element.32) | data formatting | bytes 10485760
  51.8 10.5 %copy.40 = s32[1,1,512,2560]{3,1,2,0:T(1,128)} copy(s32[1,1,512,2560]{3,2,1,0:T(8,128)} %get-tuple-element.31) | data formatting | bytes 10485760
  62.3 1.9 collective-permute-start.6
  64.2 2.7 broadcast_bitcast_fusion.2
  67.0 10.2 %copy.38 = s32[1,1,512,2560]{3,1,2,0:T(1,128)} copy(s32[1,1,512,2560]{3,2,1,0:T(8,128)} %broadcast_bitcast_fusion.2) | data formatting | bytes 10485760
  77.1 67.7 %all_gather.3 = bf16[2048,8]{1,0:T(8,128)(2,1)S(1)} all-gather(bf16[8,8]{1,0:T(8,128)(2,1)S(1)} %copy-done.17), channel_id=1, replica_groups=mesh['ctx'=32,'tp'=8] {'ctx','tp'}, dimensions={0}, use_global_device_ids=true | all-gather | bytes 32896 | tf_op jit(solution)/shard_map/all_gather | solution.py:32
  144.8 0.4 dynamic-slice_reduce_fusion
  145.2 1.9 rev.6
  147.1 0.1 concatenate.17
  147.3 0.2 tile.23
  147.5 5.8 reshape.151
  153.3 26.5 %tile.24 = bf16[1,1311232]{1,0:T(2,128)(2,1)} reshape(bf16[1311232]{0:T(1024)(128)(2,1)} %reshape.151) | data formatting | bytes 5244928 | tf_op jit(solution)/shard_map/tile | solution.py:20
  179.8 0.2 tile.26
  180.0 5.8 reshape.153
  185.8 26.6 %tile.27 = bf16[1,1311232]{1,0:T(2,128)(2,1)} reshape(bf16[1311232]{0:T(1024)(128)(2,1)} %reshape.153) | data formatting | bytes 5244928 | tf_op jit(solution)/shard_map/tile | solution.py:20
  212.5 4.6 collective-permute-start.7
  217.1 58.1 %fusion.1 = (bf16[1310720]{0:T(1024)(128)(2,1)}, bf16[1310720]{0:T(1024)(128)(2,1)S(1)}) fusion(bf16[1,1311232]{1,0:T(2,128)(2,1)} %tile.27, s32[1,1310720]{1,0:T(1,128)} %bitcast.50, s32[1,1310720]{1,0:T(1,128)} %bitcast.49, bf16[1,1311232]{1,0:T(2,128)(2,1)} %tile.24, s32[1,1310720]{1,0:T(1,128)} %bitcast.48), kind=kLoop, calls=%fused_computation.5 | loop fusion | flops 5242880 | bytes 26214400 | tf_op jit(solution)/shard_map/jit(_where)/select_n | solution.py:56
  275.2 6.1 select_n.44
  281.3 2.0 copy.30
  283.3 2.1 copy.31
  285.4 2.0 constant_dynamic-update-slice_fusion.8
  287.5 2.0 constant_dynamic-update-slice_fusion.7
  289.4 1.9 constant_dynamic-update-slice_fusion.6
  291.4 1.9 constant_dynamic-update-slice_fusion.5
  293.3 4.4 fusion.7
  297.7 0.8 copy-done.8
  298.5 1.9 collective-permute-start
  300.4 16.0 %collective-permute-done = bf16[512,512]{0,1:T(8,128)(2,1)S(1)} collective-permute-done((bf16[512,512]{0,1:T(8,128)(2,1)S(1)}, bf16[512,512]{0,1:T(8,128)(2,1)S(1)}, u32[]{:S(2)}, u32[]{:S(2)}) %collective-permute-start) | collective-permute-done | bytes 524320 | tf_op jit(solution)/shard_map/ppermute | solution.py:15
  316.4 0.8 copy-done.10
  317.2 1.9 collective-permute-start.1
  319.1 15.1 %collective-permute-done.1 = bf16[512,512]{0,1:T(8,128)(2,1)S(1)} collective-permute-done((bf16[512,512]{0,1:T(8,128)(2,1)S(1)}, bf16[512,512]{0,1:T(8,128)(2,1)S(1)}, u32[]{:S(2)}, u32[]{:S(2)}) %collective-permute-start.1) | collective-permute-done | bytes 524320 | tf_op jit(solution)/shard_map/ppermute | solution.py:15
  334.3 0.8 copy-done.12
  335.1 1.9 collective-permute-start.2
  337.0 14.4 %collective-permute-done.2 = bf16[512,512]{0,1:T(8,128)(2,1)} collective-permute-done((bf16[512,512]{0,1:T(8,128)(2,1)S(1)}, bf16[512,512]{0,1:T(8,128)(2,1)}, u32[]{:S(2)}, u32[]{:S(2)}) %collective-permute-start.2) | collective-permute-done | bytes 524320 | tf_op jit(solution)/shard_map/ppermute | solution.py:15
  351.4 1.9 collective-permute-start.3
  353.3 4.1 select_n.41
  357.4 2.1 copy.36
  359.6 2.1 copy.37
  361.7 5.3 collective-permute-done.3
  367.0 1.1 constant_dynamic-update-slice_fusion.4
  368.1 1.1 constant_dynamic-update-slice_fusion.3
  369.3 1.5 copy-done.1
  370.8 3.9 select_bitcast_fusion
  374.8 10.1 %copy.41 = f32[1,1,512,2560]{3,1,2,0:T(1,128)} copy(f32[1,1,512,2560]{3,2,1,0:T(8,128)} %select_bitcast_fusion) | data formatting | bytes 10485760
  384.9 57.9 %pad_reduce_fusion = f32[1311232]{0:T(1024)} fusion(f32[1,1310720]{1,0:T(1,128)} %bitcast.47), kind=kLoop, calls=%fused_computation.2 | loop fusion | bytes 10487808 | tf_op jit(solution)/shard_map/jit(_pad)/pad | solution.py:68
  442.8 8.6 %reshape.144 = f32[512,2561]{1,0:T(8,128)} reshape(f32[1311232]{0:T(1024)} %pad_reduce_fusion) | data formatting | bytes 10489856 | tf_op jit(solution)/shard_map/reshape | solution.py:69
  451.4 2.8 reduce_sum.11
  454.4 1.4 rev.7
  455.8 0.4 copy.33
  456.2 3.9 dynamic_update_slice.3
  460.2 1.0 copy-done
  461.2 4.3 fusion.10
  465.5 1.0 copy.34
  466.5 1.0 copy.35
  467.5 247.4 %all-reduce.5.cloned.1.call-done = f32[2048,8]{1,0:T(8,128)} async-done(((f32[2048,8]{1,0:T(8,128)}), f32[2048,8]{1,0:T(8,128)}) %all-reduce.5.cloned.1.call-update) | async-done | bytes 65552
  714.9 1.3 dynamic-slice_multiply_fusion
  (52 shorter events, 0.6 us)
Async XLA Ops:
  7.2 11.5 %copy-start.16 = (s32[16384]{0:T(1024)S(1)}, s32[16384]{0:T(1024)}, u32[]{:S(2)}) copy-start(s32[16384]{0:T(1024)} %param.11) | copy-start | bytes 196612
  7.2 707.7 %all-reduce.5.cloned.1.call-start = ((), (), s32[]{:S(2)}) async-start(), calls=%async_computation | async-start | bytes 2097152
  8.5 33.1 %copy-start.3 = (bf16[512,512]{0,1:T(8,128)(2,1)}, bf16[512,512]{0,1:T(8,128)(2,1)S(1)}, u32[]{:S(2)}) copy-start(bf16[512,512]{0,1:T(8,128)(2,1)S(1)} %copy.29) | copy-start | bytes 1572868
  9.9 31.7 %copy-start.5 = (bf16[512,512]{0,1:T(8,128)(2,1)}, bf16[512,512]{0,1:T(8,128)(2,1)S(1)}, u32[]{:S(2)}) copy-start(bf16[512,512]{0,1:T(8,128)(2,1)S(1)} %copy.32) | copy-start | bytes 1572868
  10.9 18.9 %collective-permute-start.4 = (bf16[512,512]{0,1:T(8,128)(2,1)S(1)}, bf16[512,512]{0,1:T(8,128)(2,1)S(1)}, u32[]{:S(2)}, u32[]{:S(2)}) collective-permute-start(bf16[512,512]{0,1:T(8,128)(2,1)S(1)} %get-tuple-element.23), channel_id=1, source_target_pairs={{8,0},{16,8},{24,16},{32,24},{40,32},{48,40},{56,48},{64,56},{72,6... | collective-permute-start | bytes 1572872 | tf_op jit(solution)/shard_map/ppermute | solution.py:15
  29.8 11.8 %copy-start.7 = (bf16[512,512]{0,1:T(8,128)(2,1)}, bf16[512,512]{0,1:T(8,128)(2,1)S(1)}, u32[]{:S(2)}) copy-start(bf16[512,512]{0,1:T(8,128)(2,1)S(1)} %collective-permute-done.4) | copy-start | bytes 1572868
  29.8 32.5 %collective-permute-start.5 = (bf16[512,512]{0,1:T(8,128)(2,1)S(1)}, bf16[512,512]{0,1:T(8,128)(2,1)}, u32[]{:S(2)}, u32[]{:S(2)}) collective-permute-start(bf16[512,512]{0,1:T(8,128)(2,1)S(1)} %collective-permute-done.4), channel_id=1, source_target_pairs={{8,0},{16,8},{24,16},{32,24},{40,32},{48,40},{56,48},{64,56},{72,6... | collective-permute-start | bytes 1572872 | tf_op jit(solution)/shard_map/ppermute | solution.py:15
  62.3 150.2 %collective-permute-start.6 = (bf16[512,512]{0,1:T(8,128)(2,1)}, bf16[512,512]{0,1:T(8,128)(2,1)}, u32[]{:S(2)}, u32[]{:S(2)}) collective-permute-start(bf16[512,512]{0,1:T(8,128)(2,1)} %collective-permute-done.5), channel_id=1, source_target_pairs={{8,0},{16,8},{24,16},{32,24},{40,32},{48,40},{56,48},{64,56},{72,6... | collective-permute-start | bytes 1572872 | tf_op jit(solution)/shard_map/ppermute | solution.py:15
  67.0 10.2 %copy-start.17 = (bf16[8,8]{1,0:T(8,128)(2,1)S(1)}, bf16[8,8]{1,0:T(8,128)(2,1)}, u32[]{:S(2)}) copy-start(bf16[8,8]{1,0:T(8,128)(2,1)} %param.13) | copy-start | bytes 388
  212.5 78.9 %collective-permute-start.7 = (bf16[512,512]{0,1:T(8,128)(2,1)}, bf16[512,512]{0,1:T(8,128)(2,1)}, u32[]{:S(2)}, u32[]{:S(2)}) collective-permute-start(bf16[512,512]{0,1:T(8,128)(2,1)} %collective-permute-done.6), channel_id=1, source_target_pairs={{8,0},{16,8},{24,16},{32,24},{40,32},{48,40},{56,48},{64,56},{72,6... | collective-permute-start | bytes 1572872 | tf_op jit(solution)/shard_map/ppermute | solution.py:15
  283.3 9.9 %copy-start.18 = (f32[512]{0:T(512)S(1)}, f32[512]{0:T(512)}, u32[]{:S(2)}) copy-start(f32[512]{0:T(512)} %param.12) | copy-start | bytes 6148
  285.4 7.9 %copy-start.2 = (bf16[512,2560]{1,0:T(8,128)(2,1)S(1)}, bf16[512,2560]{1,0:T(8,128)(2,1)}, u32[]{:S(2)}) copy-start(bf16[512,2560]{1,0:T(8,128)(2,1)} %select_n.44) | copy-start | bytes 7864324
  285.4 7.9 %copy-start.14 = (bf16[512,512]{0,1:T(8,128)(2,1)S(1)}, bf16[512,512]{0,1:T(8,128)(2,1)}, u32[]{:S(2)}) copy-start(bf16[512,512]{0,1:T(8,128)(2,1)} %copy.30) | copy-start | bytes 1572868
  285.4 7.9 %copy-start.15 = (bf16[512,512]{0,1:T(8,128)(2,1)S(1)}, bf16[512,512]{0,1:T(8,128)(2,1)}, u32[]{:S(2)}) copy-start(bf16[512,512]{0,1:T(8,128)(2,1)} %copy.31) | copy-start | bytes 1572868
  297.7 0.8 copy-start.8
  298.5 17.9 %collective-permute-start = (bf16[512,512]{0,1:T(8,128)(2,1)S(1)}, bf16[512,512]{0,1:T(8,128)(2,1)S(1)}, u32[]{:S(2)}, u32[]{:S(2)}) collective-permute-start(bf16[512,512]{0,1:T(8,128)(2,1)S(1)} %get-tuple-element.26), channel_id=1, source_target_pairs={{0,8},{8,16},{16,24},{24,32},{32,40},{40,48},{48,56},{56,64},{64,7... | collective-permute-start | bytes 1572872 | tf_op jit(solution)/shard_map/ppermute | solution.py:15
  316.4 0.8 copy-start.10
  317.2 17.0 %collective-permute-start.1 = (bf16[512,512]{0,1:T(8,128)(2,1)S(1)}, bf16[512,512]{0,1:T(8,128)(2,1)S(1)}, u32[]{:S(2)}, u32[]{:S(2)}) collective-permute-start(bf16[512,512]{0,1:T(8,128)(2,1)S(1)} %collective-permute-done), channel_id=1, source_target_pairs={{0,8},{8,16},{16,24},{24,32},{32,40},{40,48},{48,56},{56,64},{64,7... | collective-permute-start | bytes 1572872 | tf_op jit(solution)/shard_map/ppermute | solution.py:15
  334.3 0.8 copy-start.12
  335.1 16.3 %collective-permute-start.2 = (bf16[512,512]{0,1:T(8,128)(2,1)S(1)}, bf16[512,512]{0,1:T(8,128)(2,1)}, u32[]{:S(2)}, u32[]{:S(2)}) collective-permute-start(bf16[512,512]{0,1:T(8,128)(2,1)S(1)} %collective-permute-done.1), channel_id=1, source_target_pairs={{0,8},{8,16},{16,24},{24,32},{32,40},{40,48},{48,56},{56,64},{64,7... | collective-permute-start | bytes 1572872 | tf_op jit(solution)/shard_map/ppermute | solution.py:15
  351.4 15.6 %collective-permute-start.3 = (bf16[512,512]{0,1:T(8,128)(2,1)}, bf16[512,512]{0,1:T(8,128)(2,1)}, u32[]{:S(2)}, u32[]{:S(2)}) collective-permute-start(bf16[512,512]{0,1:T(8,128)(2,1)} %collective-permute-done.2), channel_id=1, source_target_pairs={{0,8},{8,16},{16,24},{24,32},{32,40},{40,48},{48,56},{56,64},{64,7... | collective-permute-start | bytes 1572872 | tf_op jit(solution)/shard_map/ppermute | solution.py:15
  357.4 11.8 %copy-start.13 = (bf16[512,512]{0,1:T(8,128)(2,1)S(1)}, bf16[512,512]{0,1:T(8,128)(2,1)}, u32[]{:S(2)}) copy-start(bf16[512,512]{0,1:T(8,128)(2,1)} %copy-done.12) | copy-start | bytes 1572868
  357.4 11.8 %copy-start.11 = (bf16[512,512]{0,1:T(8,128)(2,1)S(1)}, bf16[512,512]{0,1:T(8,128)(2,1)}, u32[]{:S(2)}) copy-start(bf16[512,512]{0,1:T(8,128)(2,1)} %copy-done.10) | copy-start | bytes 1572868
  359.6 9.7 %copy-start.9 = (bf16[512,512]{0,1:T(8,128)(2,1)S(1)}, bf16[512,512]{0,1:T(8,128)(2,1)}, u32[]{:S(2)}) copy-start(bf16[512,512]{0,1:T(8,128)(2,1)} %copy-done.8) | copy-start | bytes 1572868
  369.3 1.5 copy-start.1
  455.8 5.4 copy-start.4
  455.8 5.4 copy-start.6
  460.2 1.0 copy-start
Sparse Core Ops, SparseCore 0:
  461.3 253.5 all-reduce.4
where the time goes:
time: 734 us; the launch traced here: 723 us
  waiting for transfers between devices  309 us (42%)
  local copies, waits for them, and re-layouts  227 us (31%)
  blocking collectives  67.7 us (9%)
  other arithmetic  63.3 us (9%)
  starting transfers between devices  28.4 us (4%)
  between operations  14.8 us (2%)
  matrix products  12.6 us (2%)
    unnamed x2, waiting for transfers between devices  247 us
    unnamed x61, local copies, waits for them, and re-layouts  86.8 us
    all_gather x1, blocking collectives, shards(): full_taps = lax.all_gather(filter_taps, ('ctx', 'tp'), axis=0, tiled=True)  67.7 us
    ppermute x8, waiting for transfers between devices, shifted(): lax.ppermute(value, axis, [(source, source + steps) for source in range(l...  61.9 us
    select_n x1, other arithmetic, shards(): bwd_tile = jnp.where(same_rdr[None], band(bwd_window, rows, wide), 0)  58.1 us
    pad x1, local copies, waits for them, and re-layouts, shards(): jnp.pad(product.reshape(groups_here, rows * wide), ((0, 0), (0, rows)))  57.9 us
    another operation x4, local copies, waits for them, and re-layouts, band(): flat = jnp.tile(window, (1, rows))[:, :rows * cols]  53.5 us
    ppermute x8, starting transfers between devices, shifted(): lax.ppermute(value, axis, [(source, source + steps) for source in range(l...  28.4 us
  transfers between devices with their start and end apart: 9, of which 6 were waited for; matrix products, arithmetic and copies ran while one was open for 27% of the time, Pallas kernels for 0%

commit v1 on v0

--- a/solution.py
+++ b/solution.py
@@ -3,10 +3,17 @@
 import jax.numpy as jnp
 from jax import lax
 from jax.sharding import PartitionSpec as P
+from jax.lax import all_to_all, psum
 
 MAXCH = 8
 FGROUP = 512
 FLEN = 2048
+
+
+def take_the_cards(load, chip_axis):
+    y1 = jnp.stack([load] * psum(1, chip_axis))
+    m_next = all_to_all(y1, chip_axis, 0, 0)
+    return jnp.concatenate(m_next, 0)
 
 
 def shifted(value, axis, steps):
@@ -29,7 +36,7 @@
     hist = span * rows
     wide = hist + rows
     assert hist == FLEN
-    full_taps = lax.all_gather(filter_taps, ("ctx", "tp"), axis=0, tiled=True)
+    full_taps = take_the_cards(filter_taps, ("ctx", "tp"))
     first_group = lax.axis_index("tp") * groups_here
     taps = lax.dynamic_slice_in_dim(full_taps, first_group, groups_here, axis=1).T
     mixed_in = (key_in.astype(jnp.float32) * value_in.astype(jnp.float32)).astype(jnp.bfloat16)

time: 734 us -> 670 us (0.913)
  blocking collectives: 67.7 us -> 0 us
  starting transfers between devices: 28.4 us -> 42.8 us
    all_gather x1 -> x0, blocking collectives: 67.7 us -> none  [shards(): full_taps = lax.all_gather(filter_taps, ('ctx', 'tp'), axis=0, tiled=True)]
    all_to_all x0 -> x1, starting transfers between devices: none -> 9.42 us  [take_the_cards(): m_next = all_to_all(y1, chip_axis, 0, 0)]
    ppermute x8, waiting for transfers between devices: 61.9 us -> 53.7 us  [shifted(): lax.ppermute(value, axis, [(source, source + steps) for source in range(l...]
    unnamed x61 -> x66, local copies, waits for them, and re-layouts: 86.8 us -> 85 us
  transfers between devices with their start and end apart: 9 -> 10, of which waited for: 6 -> 7; matrix products, arithmetic and copies ran while one was open for 27% -> 29% of each run, Pallas kernels for 0% -> 0%
where the time goes in v1:
time: 670 us; the launch traced here: 666 us
  waiting for transfers between devices  306 us (46%)
  local copies, waits for them, and re-layouts  226 us (34%)
  other arithmetic  63.3 us (9%)
  starting transfers between devices  42.8 us (6%)
  between operations  14.6 us (2%)
  matrix products  12.6 us (2%)
    unnamed x2, waiting for transfers between devices  252 us
    unnamed x66, local copies, waits for them, and re-layouts  85 us
    select_n x1, other arithmetic, shards(): bwd_tile = jnp.where(same_rdr[None], band(bwd_window, rows, wide), 0)  58.1 us
    pad x1, local copies, waits for them, and re-layouts, shards(): jnp.pad(product.reshape(groups_here, rows * wide), ((0, 0), (0, rows)))  57.9 us
    ppermute x8, waiting for transfers between devices, shifted(): lax.ppermute(value, axis, [(source, source + steps) for source in range(l...  53.7 us
    another operation x4, local copies, waits for them, and re-layouts, band(): flat = jnp.tile(window, (1, rows))[:, :rows * cols]  53.5 us
    ppermute x8, starting transfers between devices, shifted(): lax.ppermute(value, axis, [(source, source + steps) for source in range(l...  33.3 us
  transfers between devices with their start and end apart: 10, of which 7 were waited for; matrix products, arithmetic and copies ran while one was open for 29% of the time, Pallas kernels for 0%

profile of v1, /device:TPU:2, one launch (start us, length us, event | category | flops | bytes accessed | tf_op | source)
XLA Modules:
  0.0 665.9 jit_solution(17988695364169417431)
XLA Ops:
  7.2 1.3 copy.40
  8.5 1.5 copy.45
  9.9 1.0 constant_dynamic-update-slice_fusion.9
  10.9 7.7 %collective-permute-start.4 = (bf16[512,512]{0,1:T(8,128)(2,1)S(1)}, bf16[512,512]{0,1:T(8,128)(2,1)S(1)}, u32[]{:S(2)}, u32[]{:S(2)}) collective-permute-start(bf16[512,512]{0,1:T(8,128)(2,1)S(1)} %get-tuple-element.28), channel_id=1, source_target_pairs={{8,0},{16,8},{24,16},{32,24},{40,32},{48,40},{56,48},{64,56},{72,6... | collective-permute-start | bytes 1572872 | tf_op jit(solution)/shard_map/ppermute | solution.py:22
  18.7 0.9 stack.2
  19.6 9.4 %all-to-all-start = ((bf16[256,8,8]{1,2,0:T(8,128)(2,1)}), bf16[256,8,8]{1,2,0:T(8,128)(2,1)S(1)}, u32[]{:S(2)}, u32[]{:S(2)}) async-start(bf16[256,8,8]{1,2,0:T(8,128)(2,1)} %stack.2), calls=%async_computation | async-start | bytes 1048576 | tf_op jit(solution)/shard_map/all_to_all | solution.py:15
  29.3 4.0 collective-permute-done.4
  33.3 7.5 %collective-permute-start.5 = (bf16[512,512]{0,1:T(8,128)(2,1)S(1)}, bf16[512,512]{0,1:T(8,128)(2,1)}, u32[]{:S(2)}, u32[]{:S(2)}) collective-permute-start(bf16[512,512]{0,1:T(8,128)(2,1)S(1)} %collective-permute-done.4), channel_id=1, source_target_pairs={{8,0},{16,8},{24,16},{32,24},{40,32},{48,40},{56,48},{64,56},{72,6... | collective-permute-start | bytes 1572872 | tf_op jit(solution)/shard_map/ppermute | solution.py:22
  40.8 5.2 broadcast_bitcast_fusion
  46.0 6.5 collective-permute-done.5
  52.5 6.6 collective-permute-start.6
  59.1 2.7 broadcast_bitcast_fusion.2
  61.8 10.2 %copy.52 = s32[1,1,512,2560]{3,1,2,0:T(1,128)} copy(s32[1,1,512,2560]{3,2,1,0:T(8,128)} %get-tuple-element.37) | data formatting | bytes 10485760
  72.0 10.3 %copy.53 = s32[1,1,512,2560]{3,1,2,0:T(1,128)} copy(s32[1,1,512,2560]{3,2,1,0:T(8,128)} %get-tuple-element.36) | data formatting | bytes 10485760
  82.3 10.6 %copy.51 = s32[1,1,512,2560]{3,1,2,0:T(1,128)} copy(s32[1,1,512,2560]{3,2,1,0:T(8,128)} %broadcast_bitcast_fusion.2) | data formatting | bytes 10485760
  92.9 1.0 copy.41
  93.9 1.0 copy.42
  95.0 0.7 reshape.146
  95.7 1.5 rev.6
  97.3 0.2 tile.23
  97.5 5.8 reshape.156
  103.4 26.5 %tile.24 = bf16[1,1311232]{1,0:T(2,128)(2,1)} reshape(bf16[1311232]{0:T(1024)(128)(2,1)} %reshape.156) | data formatting | bytes 5244928 | tf_op jit(solution)/shard_map/tile | solution.py:27
  129.9 0.2 tile.26
  130.1 5.8 reshape.158
  135.9 26.6 %tile.27 = bf16[1,1311232]{1,0:T(2,128)(2,1)} reshape(bf16[1311232]{0:T(1024)(128)(2,1)} %reshape.158) | data formatting | bytes 5244928 | tf_op jit(solution)/shard_map/tile | solution.py:27
  162.5 1.9 collective-permute-start.7
  164.5 58.1 %fusion.1 = (bf16[1310720]{0:T(1024)(128)(2,1)}, bf16[1310720]{0:T(1024)(128)(2,1)S(1)}) fusion(bf16[1,1311232]{1,0:T(2,128)(2,1)} %tile.27, s32[1,1310720]{1,0:T(1,128)} %bitcast.54, s32[1,1310720]{1,0:T(1,128)} %bitcast.53, bf16[1,1311232]{1,0:T(2,128)(2,1)} %tile.24, s32[1,1310720]{1,0:T(1,128)} %bitcast.52), kind=kLoop, calls=%fused_computation.5 | loop fusion | flops 5242880 | bytes 26214400 | tf_op jit(solution)/shard_map/jit(_where)/select_n | solution.py:63
  222.6 6.1 select_n.44
  228.7 2.1 constant_dynamic-update-slice_fusion.8
  230.8 1.9 constant_dynamic-update-slice_fusion.7
  232.6 2.0 constant_dynamic-update-slice_fusion.6
  234.6 1.9 constant_dynamic-update-slice_fusion.5
  236.6 4.4 fusion.7
  241.0 0.8 copy-done.10
  241.8 3.9 collective-permute-start
  245.7 12.6 %collective-permute-done = bf16[512,512]{0,1:T(8,128)(2,1)S(1)} collective-permute-done((bf16[512,512]{0,1:T(8,128)(2,1)S(1)}, bf16[512,512]{0,1:T(8,128)(2,1)S(1)}, u32[]{:S(2)}, u32[]{:S(2)}) %collective-permute-start) | collective-permute-done | bytes 524320 | tf_op jit(solution)/shard_map/ppermute | solution.py:22
  258.3 0.8 copy-done.14
  259.1 1.9 collective-permute-start.1
  261.0 13.7 %collective-permute-done.1 = bf16[512,512]{0,1:T(8,128)(2,1)S(1)} collective-permute-done((bf16[512,512]{0,1:T(8,128)(2,1)S(1)}, bf16[512,512]{0,1:T(8,128)(2,1)S(1)}, u32[]{:S(2)}, u32[]{:S(2)}) %collective-permute-start.1) | collective-permute-done | bytes 524320 | tf_op jit(solution)/shard_map/ppermute | solution.py:22
  274.7 0.8 copy-done.16
  275.5 1.9 collective-permute-start.2
  277.4 13.0 %collective-permute-done.2 = bf16[512,512]{0,1:T(8,128)(2,1)} collective-permute-done((bf16[512,512]{0,1:T(8,128)(2,1)S(1)}, bf16[512,512]{0,1:T(8,128)(2,1)}, u32[]{:S(2)}, u32[]{:S(2)}) %collective-permute-start.2) | collective-permute-done | bytes 524320 | tf_op jit(solution)/shard_map/ppermute | solution.py:22
  290.4 1.9 collective-permute-start.3
  292.3 4.1 select_n.41
  296.4 2.1 copy.49
  298.6 2.1 copy.50
  300.7 4.0 collective-permute-done.3
  304.6 1.1 constant_dynamic-update-slice_fusion.4
  305.7 1.1 constant_dynamic-update-slice_fusion.3
  307.0 1.5 copy-done.1
  308.5 3.9 select_bitcast_fusion
  312.4 10.2 %copy.54 = f32[1,1,512,2560]{3,1,2,0:T(1,128)} copy(f32[1,1,512,2560]{3,2,1,0:T(8,128)} %select_bitcast_fusion) | data formatting | bytes 10485760
  322.6 57.9 %pad_reduce_fusion = f32[1311232]{0:T(1024)} fusion(f32[1,1310720]{1,0:T(1,128)} %bitcast.51), kind=kLoop, calls=%fused_computation.2 | loop fusion | bytes 10487808 | tf_op jit(solution)/shard_map/jit(_pad)/pad | solution.py:75
  380.5 8.6 %reshape.150 = f32[512,2561]{1,0:T(8,128)} reshape(f32[1311232]{0:T(1024)} %pad_reduce_fusion) | data formatting | bytes 10489856 | tf_op jit(solution)/shard_map/reshape | solution.py:76
  389.1 2.8 reduce_sum.11
  392.0 1.4 rev.7
  393.5 0.4 copy.46
  393.9 3.9 dynamic_update_slice.3
  397.9 1.0 copy-done
  398.9 4.3 fusion.10
  403.1 1.0 copy.47
  404.1 1.0 copy.48
  405.2 252.4 %all-reduce.5.cloned.1.call-done = f32[2048,8]{1,0:T(8,128)} async-done(((f32[2048,8]{1,0:T(8,128)}), f32[2048,8]{1,0:T(8,128)}) %all-reduce.5.cloned.1.call-update) | async-done | bytes 65552
  657.5 1.3 dynamic-slice_multiply_fusion
  (60 shorter events, 1.0 us)
Async XLA Ops:
  7.2 11.5 %copy-start.19 = (bf16[8,8]{1,0:T(8,128)(2,1)S(1)}, bf16[8,8]{1,0:T(8,128)(2,1)}, u32[]{:S(2)}) copy-start(bf16[8,8]{1,0:T(8,128)(2,1)} %param.13) | copy-start | bytes 388
  8.4 11.2 %copy-start.3 = (bf16[512,512]{0,1:T(8,128)(2,1)}, bf16[512,512]{0,1:T(8,128)(2,1)S(1)}, u32[]{:S(2)}) copy-start(bf16[512,512]{0,1:T(8,128)(2,1)S(1)} %copy.40) | copy-start | bytes 1572868
  8.4 20.6 %copy-start.18 = (s32[16384]{0:T(1024)S(1)}, s32[16384]{0:T(1024)}, u32[]{:S(2)}) copy-start(s32[16384]{0:T(1024)} %param.11) | copy-start | bytes 196612
  9.9 36.1 %copy-start.5 = (bf16[512,512]{0,1:T(8,128)(2,1)}, bf16[512,512]{0,1:T(8,128)(2,1)S(1)}, u32[]{:S(2)}) copy-start(bf16[512,512]{0,1:T(8,128)(2,1)S(1)} %copy.45) | copy-start | bytes 1572868
  10.9 22.4 %collective-permute-start.4 = (bf16[512,512]{0,1:T(8,128)(2,1)S(1)}, bf16[512,512]{0,1:T(8,128)(2,1)S(1)}, u32[]{:S(2)}, u32[]{:S(2)}) collective-permute-start(bf16[512,512]{0,1:T(8,128)(2,1)S(1)} %get-tuple-element.28), channel_id=1, source_target_pairs={{8,0},{16,8},{24,16},{32,24},{40,32},{48,40},{56,48},{64,56},{72,6... | collective-permute-start | bytes 1572872 | tf_op jit(solution)/shard_map/ppermute | solution.py:22
  19.6 75.3 %all-to-all-start = ((bf16[256,8,8]{1,2,0:T(8,128)(2,1)}), bf16[256,8,8]{1,2,0:T(8,128)(2,1)S(1)}, u32[]{:S(2)}, u32[]{:S(2)}) async-start(bf16[256,8,8]{1,2,0:T(8,128)(2,1)} %stack.2), calls=%async_computation | async-start | bytes 1048576 | tf_op jit(solution)/shard_map/all_to_all | solution.py:15
  29.0 628.5 %all-reduce.5.cloned.1.call-start = ((), (), s32[]{:S(2)}) async-start(), calls=%async_computation.1 | async-start | bytes 2097152
  33.3 12.8 %copy-start.9 = (bf16[512,512]{0,1:T(8,128)(2,1)}, bf16[512,512]{0,1:T(8,128)(2,1)S(1)}, u32[]{:S(2)}) copy-start(bf16[512,512]{0,1:T(8,128)(2,1)S(1)} %collective-permute-done.4) | copy-start | bytes 1572868
  33.3 19.2 %collective-permute-start.5 = (bf16[512,512]{0,1:T(8,128)(2,1)S(1)}, bf16[512,512]{0,1:T(8,128)(2,1)}, u32[]{:S(2)}, u32[]{:S(2)}) collective-permute-start(bf16[512,512]{0,1:T(8,128)(2,1)S(1)} %collective-permute-done.4), channel_id=1, source_target_pairs={{8,0},{16,8},{24,16},{32,24},{40,32},{48,40},{56,48},{64,56},{72,6... | collective-permute-start | bytes 1572872 | tf_op jit(solution)/shard_map/ppermute | solution.py:22
  52.5 110.0 %collective-permute-start.6 = (bf16[512,512]{0,1:T(8,128)(2,1)}, bf16[512,512]{0,1:T(8,128)(2,1)}, u32[]{:S(2)}, u32[]{:S(2)}) collective-permute-start(bf16[512,512]{0,1:T(8,128)(2,1)} %collective-permute-done.5), channel_id=1, source_target_pairs={{8,0},{16,8},{24,16},{32,24},{40,32},{48,40},{56,48},{64,56},{72,6... | collective-permute-start | bytes 1572872 | tf_op jit(solution)/shard_map/ppermute | solution.py:22
  82.3 10.6 %copy-start.7 = (bf16[512,512]{1,0:T(8,128)(2,1)S(1)}, bf16[512,512]{1,0:T(8,128)(2,1)}, u32[]{:S(2)}) copy-start(bf16[512,512]{1,0:T(8,128)(2,1)} %param.8) | copy-start | bytes 1572868
  82.3 11.6 %copy-start.8 = (bf16[512,512]{1,0:T(8,128)(2,1)S(1)}, bf16[512,512]{1,0:T(8,128)(2,1)}, u32[]{:S(2)}) copy-start(bf16[512,512]{1,0:T(8,128)(2,1)} %param.9) | copy-start | bytes 1572868
  162.5 72.1 %collective-permute-start.7 = (bf16[512,512]{0,1:T(8,128)(2,1)}, bf16[512,512]{0,1:T(8,128)(2,1)}, u32[]{:S(2)}, u32[]{:S(2)}) collective-permute-start(bf16[512,512]{0,1:T(8,128)(2,1)} %collective-permute-done.6), channel_id=1, source_target_pairs={{8,0},{16,8},{24,16},{32,24},{40,32},{48,40},{56,48},{64,56},{72,6... | collective-permute-start | bytes 1572872 | tf_op jit(solution)/shard_map/ppermute | solution.py:22
  228.7 7.9 %copy-start.2 = (bf16[512,2560]{1,0:T(8,128)(2,1)S(1)}, bf16[512,2560]{1,0:T(8,128)(2,1)}, u32[]{:S(2)}) copy-start(bf16[512,2560]{1,0:T(8,128)(2,1)} %select_n.44) | copy-start | bytes 7864324
  228.7 7.9 %copy-start.12 = (bf16[512,512]{0,1:T(8,128)(2,1)S(1)}, bf16[512,512]{0,1:T(8,128)(2,1)}, u32[]{:S(2)}) copy-start(bf16[512,512]{0,1:T(8,128)(2,1)} %copy.41) | copy-start | bytes 1572868
  228.7 7.9 %copy-start.13 = (bf16[512,512]{0,1:T(8,128)(2,1)S(1)}, bf16[512,512]{0,1:T(8,128)(2,1)}, u32[]{:S(2)}) copy-start(bf16[512,512]{0,1:T(8,128)(2,1)} %copy.42) | copy-start | bytes 1572868
  228.7 7.9 %copy-start.20 = (f32[512]{0:T(512)S(1)}, f32[512]{0:T(512)}, u32[]{:S(2)}) copy-start(f32[512]{0:T(512)} %param.12) | copy-start | bytes 6148
  241.0 0.8 copy-start.10
  241.8 16.5 %collective-permute-start = (bf16[512,512]{0,1:T(8,128)(2,1)S(1)}, bf16[512,512]{0,1:T(8,128)(2,1)S(1)}, u32[]{:S(2)}, u32[]{:S(2)}) collective-permute-start(bf16[512,512]{0,1:T(8,128)(2,1)S(1)} %get-tuple-element.31), channel_id=1, source_target_pairs={{0,8},{8,16},{16,24},{24,32},{32,40},{40,48},{48,56},{56,64},{64,7... | collective-permute-start | bytes 1572872 | tf_op jit(solution)/shard_map/ppermute | solution.py:22
  258.3 0.8 copy-start.14
  259.1 15.6 %collective-permute-start.1 = (bf16[512,512]{0,1:T(8,128)(2,1)S(1)}, bf16[512,512]{0,1:T(8,128)(2,1)S(1)}, u32[]{:S(2)}, u32[]{:S(2)}) collective-permute-start(bf16[512,512]{0,1:T(8,128)(2,1)S(1)} %collective-permute-done), channel_id=1, source_target_pairs={{0,8},{8,16},{16,24},{24,32},{32,40},{40,48},{48,56},{56,64},{64,7... | collective-permute-start | bytes 1572872 | tf_op jit(solution)/shard_map/ppermute | solution.py:22
  274.7 0.8 copy-start.16
  275.5 14.9 %collective-permute-start.2 = (bf16[512,512]{0,1:T(8,128)(2,1)S(1)}, bf16[512,512]{0,1:T(8,128)(2,1)}, u32[]{:S(2)}, u32[]{:S(2)}) collective-permute-start(bf16[512,512]{0,1:T(8,128)(2,1)S(1)} %collective-permute-done.1), channel_id=1, source_target_pairs={{0,8},{8,16},{16,24},{24,32},{32,40},{40,48},{48,56},{56,64},{64,7... | collective-permute-start | bytes 1572872 | tf_op jit(solution)/shard_map/ppermute | solution.py:22
  290.4 14.2 %collective-permute-start.3 = (bf16[512,512]{0,1:T(8,128)(2,1)}, bf16[512,512]{0,1:T(8,128)(2,1)}, u32[]{:S(2)}, u32[]{:S(2)}) collective-permute-start(bf16[512,512]{0,1:T(8,128)(2,1)} %collective-permute-done.2), channel_id=1, source_target_pairs={{0,8},{8,16},{16,24},{24,32},{32,40},{40,48},{48,56},{56,64},{64,7... | collective-permute-start | bytes 1572872 | tf_op jit(solution)/shard_map/ppermute | solution.py:22
  296.4 10.4 %copy-start.17 = (bf16[512,512]{0,1:T(8,128)(2,1)S(1)}, bf16[512,512]{0,1:T(8,128)(2,1)}, u32[]{:S(2)}) copy-start(bf16[512,512]{0,1:T(8,128)(2,1)} %copy-done.16) | copy-start | bytes 1572868
  296.4 10.4 %copy-start.15 = (bf16[512,512]{0,1:T(8,128)(2,1)S(1)}, bf16[512,512]{0,1:T(8,128)(2,1)}, u32[]{:S(2)}) copy-start(bf16[512,512]{0,1:T(8,128)(2,1)} %copy-done.14) | copy-start | bytes 1572868
  298.6 8.3 %copy-start.11 = (bf16[512,512]{0,1:T(8,128)(2,1)S(1)}, bf16[512,512]{0,1:T(8,128)(2,1)}, u32[]{:S(2)}) copy-start(bf16[512,512]{0,1:T(8,128)(2,1)} %copy-done.10) | copy-start | bytes 1572868
  307.0 1.5 copy-start.1
  393.5 5.4 copy-start.4
  393.5 5.4 copy-start.6
  397.9 1.0 copy-start
Sparse Core Ops, SparseCore 0:
  399.0 258.5 all-reduce.4
